TPU v7x, 32 devices: a whole 2x2x4 slice. The times are simulated.
32 devices in a mesh: section: 2 (over x), tm: 4 (over z), space: 4 (over y, core).
Axes of the slice: x: 2, y: 2, z: 4, core: 2. Of those that a mesh axis runs over, the one named last changes fastest.
Arguments:
- video: bfloat16 [2, 8, 16, 512, 128], P('section', 'tm', 'space'), may hold values from -6 to 6
- weights: bfloat16 [2, 9, 384, 128], P('section'), may hold values from -0.109375 to 0.109375
Outputs:
- decoded: bfloat16 [2, 8, 16, 512, 128], P('section', 'tm', 'space')
All inputs are finite; a program needn't handle non-finite values.
Results may differ from a plain program's by a relative error of at most 0.0095.
Values may be sent and summed in bfloat16 or wider, within the bound.
No kernel may reach another device: no remote copies, remote signals or barrier semaphores. Data moves between devices by JAX's collectives and lax.ppermute only.
A program may use at most 128 MiB of HBM per device.

v0:
```python
import jax
import jax.numpy as jnp
from jax import lax
from jax.sharding import PartitionSpec as P


def from_behind(block, axis, distance):
    devices = range(lax.axis_size(axis))
    route = [(i - distance, i) for i in devices if i - distance in devices]
    return lax.ppermute(block, axis, route)


def padded_2(cells, sides, width):
    for axis, dim in sides:
        count = lax.axis_size(axis)
        ends = count - 1
        head = lax.slice_in_dim(cells, 0, width, axis=dim)
        tail = lax.slice_in_dim(cells, cells.shape[dim] - width, cells.shape[dim], axis=dim)
        cells = jnp.concatenate(
            [
                lax.ppermute(tail, axis, [(i, (i + 1) % count) for i in range(ends)]),
                cells,
                lax.ppermute(head, axis, [((i + 1) % count, i) for i in range(ends)]),
            ],
            axis=dim,
        )
    return cells


def conv_block(clip, taps):
    frames, rows, width, chans = clip.shape
    act = jax.nn.silu(clip.astype(jnp.float32)).astype(jnp.bfloat16)
    carried = from_behind(act, "tm", 1)
    extended = jnp.concatenate([carried, act], axis=0)
    padded = padded_2(extended, (("space", 1),), 1)
    padded = jnp.pad(padded, ((0, 0), (0, 0), (1, 1), (0, 0)))
    joined = jnp.concatenate(
        [padded[:, :, 0:width], padded[:, :, 1 : width + 1], padded[:, :, 2 : width + 2]], axis=-1
    )
    total = jnp.zeros((frames * rows * width, chans), jnp.float32)
    for time_tap in range(3):
        for row_tap in range(3):
            slab = joined[time_tap : time_tap + frames, row_tap : row_tap + rows]
            total = total + jnp.dot(
                slab.reshape(-1, 3 * chans),
                taps[time_tap * 3 + row_tap],
                preferred_element_type=jnp.float32,
            )
    return (clip.astype(jnp.float32) + total.reshape(clip.shape)).astype(jnp.bfloat16)


def body(video, weights):
    all_taps = lax.all_gather(weights, "section", axis=0, tiled=True)
    first_taps = all_taps[0]
    second_taps = all_taps[1]
    index = 0
    hiddens = [conv_block(video[index], first_taps)]
    index = 0
    finished = [conv_block(hiddens[index], second_taps)]
    return jnp.stack(finished, axis=0)


def solution(mesh):
    return jax.shard_map(
        body,
        mesh=mesh,
        in_specs=(P("section", "tm", "space", None, None), P("section", None, None, None)),
        out_specs=P("section", "tm", "space", None, None),
        check_vma=False,
    )
```

profile of v0, /device:TPU:1, one launch (start us, length us, event | category | flops | bytes accessed | tf_op | source)
XLA Modules:
  0.0 177.2 jit_solution(865191045750303736)
XLA Ops:
  6.5 0.0 all-gather.2.cloned.1.call-start
  6.5 1.8 %fusion.24 = bf16[2,4,512,128]{3,2,1,0:T(8,128)(2,1)S(1)} fusion(bf16[1,2,4,512,128]{4,3,2,1,0:T(8,128)(2,1)} %param.2), kind=kLoop, calls=%fused_computation.39 | loop fusion | flops 3145728 | bytes 2097152 | tf_op jit(solution)/shard_map/convert_element_type | solution.py:32
  8.3 4.1 %collective-permute-start = (bf16[2,4,512,128]{3,2,1,0:T(8,128)(2,1)S(1)}, bf16[2,4,512,128]{3,2,1,0:T(8,128)(2,1)S(1)}, u32[]{:S(2)}, u32[]{:S(2)}) collective-permute-start(bf16[2,4,512,128]{3,2,1,0:T(8,128)(2,1)S(1)} %fusion.24), channel_id=1, source_target_pairs={{0,4},{4,8},{8,12},{1,5},{5,9},{9,13},{2,6},{6,10},{10,14},{3,7},{... | collective-permute-start | bytes 3145736 | tf_op jit(solution)/shard_map/ppermute | solution.py:10
  12.4 21.7 %collective-permute-done = bf16[2,4,512,128]{3,2,1,0:T(8,128)(2,1)S(1)} collective-permute-done((bf16[2,4,512,128]{3,2,1,0:T(8,128)(2,1)S(1)}, bf16[2,4,512,128]{3,2,1,0:T(8,128)(2,1)S(1)}, u32[]{:S(2)}, u32[]{:S(2)}) %collective-permute-start) | collective-permute-done | bytes 1048608 | tf_op jit(solution)/shard_map/ppermute | solution.py:10
  34.2 1.1 pad_maximum_fusion.5
  35.2 4.6 %collective-permute-start.1 = (bf16[4,1,512,128]{3,2,1,0:T(8,128)(2,1)}, bf16[4,1,512,128]{3,2,1,0:T(8,128)(2,1)S(1)}, u32[]{:S(2)}, u32[]{:S(2)}) collective-permute-start(bf16[4,1,512,128]{3,2,1,0:T(8,128)(2,1)} %get-tuple-element.29), channel_id=1, source_target_pairs={{0,1},{1,2},{2,3},{4,5},{5,6},{6,7},{8,9},{9,10},{10,11},{12,13},{... | collective-permute-start | bytes 1572872 | tf_op jit(solution)/shard_map/ppermute | solution.py:21
  39.8 1.9 %collective-permute-start.2 = (bf16[4,1,512,128]{3,2,1,0:T(8,128)(2,1)}, bf16[4,1,512,128]{3,2,1,0:T(8,128)(2,1)S(1)}, u32[]{:S(2)}, u32[]{:S(2)}) collective-permute-start(bf16[4,1,512,128]{3,2,1,0:T(8,128)(2,1)} %get-tuple-element.30), channel_id=1, source_target_pairs={{1,0},{2,1},{3,2},{5,4},{6,5},{7,6},{9,8},{10,9},{11,10},{13,12},{... | collective-permute-start | bytes 1572872 | tf_op jit(solution)/shard_map/ppermute | solution.py:23
  41.7 0.0 all-gather.2.cloned.1.call-update
  41.8 4.5 %collective-permute-done.1 = bf16[4,1,512,128]{3,2,1,0:T(8,128)(2,1)S(1)} collective-permute-done((bf16[4,1,512,128]{3,2,1,0:T(8,128)(2,1)}, bf16[4,1,512,128]{3,2,1,0:T(8,128)(2,1)S(1)}, u32[]{:S(2)}, u32[]{:S(2)}) %collective-permute-start.1) | collective-permute-done | bytes 524320 | tf_op jit(solution)/shard_map/ppermute | solution.py:21
  46.2 4.3 %collective-permute-done.2 = bf16[4,1,512,128]{3,2,1,0:T(8,128)(2,1)S(1)} collective-permute-done((bf16[4,1,512,128]{3,2,1,0:T(8,128)(2,1)}, bf16[4,1,512,128]{3,2,1,0:T(8,128)(2,1)S(1)}, u32[]{:S(2)}, u32[]{:S(2)}) %collective-permute-start.2) | collective-permute-done | bytes 524320 | tf_op jit(solution)/shard_map/ppermute | solution.py:23
  50.5 1.9 %select_maximum_fusion.3 = bf16[4,6,514,128]{3,2,1,0:T(8,128)(2,1)S(1)} fusion(bf16[4,1,512,128]{3,2,1,0:T(8,128)(2,1)S(1)} %collective-permute-done.2, bf16[4,1,512,128]{3,2,1,0:T(8,128)(2,1)S(1)} %collective-permute-done.1, bf16[2,4,512,128]{3,2,1,0:T(8,128)(2,1)S(1)} %fusion.24, bf16[2,4,512,128]{3,2,1,0:T(8,128)(2,1)S(1)} %collective-permute-done), kind=kLoop, calls=%fused_computation.24 | loop fusion | flops 23685120 | bytes 6303744 | tf_op jit(solution)/shard_map/concatenate | solution.py:19
  52.4 2.3 %fusion.50 = (bf16[4,6,512,128]{3,2,1,0:T(8,128)(2,1)S(1)}, bf16[4,6,512,128]{3,2,1,0:T(8,128)(2,1)S(1)}) fusion(bf16[4,6,514,128]{3,2,1,0:T(8,128)(2,1)S(1)} %select_maximum_fusion.3), kind=kLoop, calls=%fused_computation.88 | loop fusion | bytes 12582912 | tf_op jit(solution)/shard_map/slice | solution.py:38
  54.7 1.7 pad_maximum_fusion
  56.5 9.3 %fusion.48 = (bf16[2,4,512,384]{3,2,1,0:T(8,128)(2,1)}, bf16[2,4,512,384]{3,2,1,0:T(8,128)(2,1)}, bf16[2,4,512,384]{3,2,1,0:T(8,128)(2,1)}, bf16[2,4,512,384]{3,...) fusion(bf16[4,6,512,384]{3,2,1,0:T(8,128)(2,1)S(1)} %pad_maximu, ...), kind=kLoop, calls=%fused_computation.86 | loop fusion | bytes 56623104 | tf_op jit(solution)/shard_map/slice | solution.py:43
  65.7 7.7 %all-gather.2.cloned.1.call-done = bf16[2,9,384,128]{3,2,1,0:T(8,128)(2,1)} async-done(((bf16[1,9,384,128]{3,2,1,0:T(8,128)(2,1)}), bf16[2,9,384,128]{3,2,1,0:T(8,128)(2,1)}) %all-gather.2.cloned.1.call-update) | async-done | bytes 1769488 | tf_op jit(solution)/shard_map/all_gather | solution.py:53
  73.4 3.0 %fusion.39 = f32[4096,128]{1,0:T(8,128)S(1)} fusion(bf16[4096,384]{1,0:T(8,128)(2,1)} %bitcast.128, bf16[2,9,384,128]{3,2,1,0:T(8,128)(2,1)} %all-gather.2.cloned.1.call-done), kind=kOutput, calls=%fused_computation.69 | convolution fusion | flops 402653184 | bytes 5341184 | tf_op jit(solution)/shard_map/dot_general | solution.py:44
  76.5 0.0 copy-done.7
  76.5 0.0 copy-start.5
  76.5 2.0 %fusion.40 = f32[4096,128]{1,0:T(8,128)S(1)} fusion(bf16[4096,384]{1,0:T(8,128)(2,1)S(1)} %bitcast.126, bf16[2,9,384,128]{3,2,1,0:T(8,128)(2,1)} %all-gather.2.cloned.1.call-done), kind=kOutput, calls=%fused_computation.71 | convolution fusion | flops 402653184 | bytes 5341184 | tf_op jit(solution)/shard_map/dot_general | solution.py:44
  78.5 0.0 copy-done.5
  78.5 0.0 copy-start.3
  78.5 2.0 %fusion.41 = f32[4096,128]{1,0:T(8,128)S(1)} fusion(bf16[4096,384]{1,0:T(8,128)(2,1)S(1)} %bitcast.124, bf16[2,9,384,128]{3,2,1,0:T(8,128)(2,1)} %all-gather.2.cloned.1.call-done), kind=kOutput, calls=%fused_computation.73 | convolution fusion | flops 402653184 | bytes 5341184 | tf_op jit(solution)/shard_map/dot_general | solution.py:44
  80.6 0.0 copy-done.3
  80.6 0.0 copy-start.2
  80.6 2.0 %fusion.42 = f32[4096,128]{1,0:T(8,128)S(1)} fusion(bf16[4096,384]{1,0:T(8,128)(2,1)S(1)} %bitcast.122, bf16[2,9,384,128]{3,2,1,0:T(8,128)(2,1)} %all-gather.2.cloned.1.call-done), kind=kOutput, calls=%fused_computation.75 | convolution fusion | flops 402653184 | bytes 5341184 | tf_op jit(solution)/shard_map/dot_general | solution.py:44
  82.6 0.0 copy-done.2
  82.6 0.0 copy-start.1
  82.6 2.0 %fusion.43 = f32[4096,128]{1,0:T(8,128)S(1)} fusion(bf16[4096,384]{1,0:T(8,128)(2,1)S(1)} %bitcast.120, bf16[2,9,384,128]{3,2,1,0:T(8,128)(2,1)} %all-gather.2.cloned.1.call-done), kind=kOutput, calls=%fused_computation.77 | convolution fusion | flops 402653184 | bytes 5341184 | tf_op jit(solution)/shard_map/dot_general | solution.py:44
  84.7 0.0 copy-done.1
  84.7 0.0 copy-start
  84.7 2.0 %fusion.44 = f32[4096,128]{1,0:T(8,128)S(1)} fusion(bf16[4096,384]{1,0:T(8,128)(2,1)S(1)} %bitcast.119, bf16[2,9,384,128]{3,2,1,0:T(8,128)(2,1)} %all-gather.2.cloned.1.call-done), kind=kOutput, calls=%fused_computation.79 | convolution fusion | flops 402653184 | bytes 5341184 | tf_op jit(solution)/shard_map/dot_general | solution.py:44
  86.7 0.0 copy-done
  86.7 1.9 %fusion.45 = f32[4096,128]{1,0:T(8,128)S(1)} fusion(bf16[4096,384]{1,0:T(8,128)(2,1)S(1)} %bitcast.118, bf16[2,9,384,128]{3,2,1,0:T(8,128)(2,1)} %all-gather.2.cloned.1.call-done), kind=kOutput, calls=%fused_computation.81 | convolution fusion | flops 402653184 | bytes 5341184 | tf_op jit(solution)/shard_map/dot_general | solution.py:44
  88.6 0.0 copy-start.12
  88.6 2.0 %fusion.46 = f32[4096,128]{1,0:T(8,128)S(1)} fusion(bf16[4096,384]{1,0:T(8,128)(2,1)S(1)} %bitcast.117, bf16[2,9,384,128]{3,2,1,0:T(8,128)(2,1)} %all-gather.2.cloned.1.call-done), kind=kOutput, calls=%fused_computation.83 | convolution fusion | flops 402653184 | bytes 5341184 | tf_op jit(solution)/shard_map/dot_general | solution.py:44
  90.6 0.0 copy-done.12
  90.6 0.0 copy-start.14
  90.6 2.8 %fusion.14 = f32[4096,128]{1,0:T(8,128)S(1)} fusion(f32[4096,128]{1,0:T(8,128)S(1)} %fusion.39, f32[4096,128]{1,0:T(8,128)S(1)} %fusion.40, f32[4096,128]{1,0:T(8,128)S(1)} %fusion.41, f32[4096,128]{1,0:T(8,128)S(1)} %fusion.42, f32[4096,128]{1,0:T(8,128)S(1)} %fusion.43, f32[4096,128]{1,0:T(8,128)S(1)} %fusion.44, f32[4096,128]{1,0:T(8,128)S(1)} %fusion.45, ...), kind=kOutput, calls=%fused_computation.20 | convolution fusion | flops 406847488 | bytes 22118400 | tf_op jit(solution)/shard_map/dot_general | solution.py:44
  93.5 0.0 copy-done.14
  93.5 0.6 fusion.30
  94.0 3.2 %collective-permute-start.3 = (bf16[2,4,512,128]{3,2,1,0:T(8,128)(2,1)S(1)}, bf16[2,4,512,128]{3,2,1,0:T(8,128)(2,1)S(1)}, u32[]{:S(2)}, u32[]{:S(2)}) collective-permute-start(bf16[2,4,512,128]{3,2,1,0:T(8,128)(2,1)S(1)} %fusion.30), channel_id=1, source_target_pairs={{0,4},{4,8},{8,12},{1,5},{5,9},{9,13},{2,6},{6,10},{10,14},{3,7},{... | collective-permute-start | bytes 3145736 | tf_op jit(solution)/shard_map/ppermute | solution.py:10
  97.2 21.8 %collective-permute-done.3 = bf16[2,4,512,128]{3,2,1,0:T(8,128)(2,1)S(1)} collective-permute-done((bf16[2,4,512,128]{3,2,1,0:T(8,128)(2,1)S(1)}, bf16[2,4,512,128]{3,2,1,0:T(8,128)(2,1)S(1)}, u32[]{:S(2)}, u32[]{:S(2)}) %collective-permute-start.3) | collective-permute-done | bytes 1048608 | tf_op jit(solution)/shard_map/ppermute | solution.py:10
  119.0 0.1 pad_maximum_fusion.3
  119.1 4.5 %collective-permute-start.4 = (bf16[4,1,512,128]{3,2,1,0:T(8,128)(2,1)S(1)}, bf16[4,1,512,128]{3,2,1,0:T(8,128)(2,1)S(1)}, u32[]{:S(2)}, u32[]{:S(2)}) collective-permute-start(bf16[4,1,512,128]{3,2,1,0:T(8,128)(2,1)S(1)} %get-tuple-element.27), channel_id=1, source_target_pairs={{0,1},{1,2},{2,3},{4,5},{5,6},{6,7},{8,9},{9,10},{10,11},{12,13},{... | collective-permute-start | bytes 1572872 | tf_op jit(solution)/shard_map/ppermute | solution.py:21
  123.6 1.9 %collective-permute-start.5 = (bf16[4,1,512,128]{3,2,1,0:T(8,128)(2,1)S(1)}, bf16[4,1,512,128]{3,2,1,0:T(8,128)(2,1)S(1)}, u32[]{:S(2)}, u32[]{:S(2)}) collective-permute-start(bf16[4,1,512,128]{3,2,1,0:T(8,128)(2,1)S(1)} %get-tuple-element.28), channel_id=1, source_target_pairs={{1,0},{2,1},{3,2},{5,4},{6,5},{7,6},{9,8},{10,9},{11,10},{13,12},{... | collective-permute-start | bytes 1572872 | tf_op jit(solution)/shard_map/ppermute | solution.py:23
  125.5 4.2 %collective-permute-done.4 = bf16[4,1,512,128]{3,2,1,0:T(8,128)(2,1)S(1)} collective-permute-done((bf16[4,1,512,128]{3,2,1,0:T(8,128)(2,1)S(1)}, bf16[4,1,512,128]{3,2,1,0:T(8,128)(2,1)S(1)}, u32[]{:S(2)}, u32[]{:S(2)}) %collective-permute-start.4) | collective-permute-done | bytes 524320 | tf_op jit(solution)/shard_map/ppermute | solution.py:21
  129.7 4.4 %collective-permute-done.5 = bf16[4,1,512,128]{3,2,1,0:T(8,128)(2,1)S(1)} collective-permute-done((bf16[4,1,512,128]{3,2,1,0:T(8,128)(2,1)S(1)}, bf16[4,1,512,128]{3,2,1,0:T(8,128)(2,1)S(1)}, u32[]{:S(2)}, u32[]{:S(2)}) %collective-permute-start.5) | collective-permute-done | bytes 524320 | tf_op jit(solution)/shard_map/ppermute | solution.py:23
  134.1 1.9 %select_maximum_fusion = bf16[4,6,514,128]{3,2,1,0:T(8,128)(2,1)S(1)} fusion(bf16[4,1,512,128]{3,2,1,0:T(8,128)(2,1)S(1)} %collective-permute-done.5, bf16[4,1,512,128]{3,2,1,0:T(8,128)(2,1)S(1)} %collective-permute-done.4, bf16[2,4,512,128]{3,2,1,0:T(8,128)(2,1)S(1)} %fusion.30, bf16[2,4,512,128]{3,2,1,0:T(8,128)(2,1)S(1)} %collective-permute-done.3), kind=kLoop, calls=%fused_computation.21 | loop fusion | flops 23685120 | bytes 6303744 | tf_op jit(solution)/shard_map/concatenate | solution.py:19
  136.0 2.3 %fusion.49 = (bf16[4,6,512,128]{3,2,1,0:T(8,128)(2,1)S(1)}, bf16[4,6,512,128]{3,2,1,0:T(8,128)(2,1)S(1)}) fusion(bf16[4,6,514,128]{3,2,1,0:T(8,128)(2,1)S(1)} %select_maximum_fusion), kind=kLoop, calls=%fused_computation.87 | loop fusion | bytes 12582912 | tf_op jit(solution)/shard_map/slice | solution.py:38
  138.3 1.7 pad_maximum_fusion.1
  140.0 9.3 %fusion.47 = (bf16[2,4,512,384]{3,2,1,0:T(8,128)(2,1)}, bf16[2,4,512,384]{3,2,1,0:T(8,128)(2,1)}, bf16[2,4,512,384]{3,2,1,0:T(8,128)(2,1)}, bf16[2,4,512,384]{3,...) fusion(bf16[4,6,512,384]{3,2,1,0:T(8,128)(2,1)S(1)} %pad_maximu, ...), kind=kLoop, calls=%fused_computation.85 | loop fusion | bytes 56623104 | tf_op jit(solution)/shard_map/slice | solution.py:43
  149.4 3.0 %fusion.31 = f32[4096,128]{1,0:T(8,128)S(1)} fusion(bf16[4096,384]{1,0:T(8,128)(2,1)} %bitcast.132, bf16[2,9,384,128]{3,2,1,0:T(8,128)(2,1)} %all-gather.2.cloned.1.call-done), kind=kOutput, calls=%fused_computation.52 | convolution fusion | flops 402653184 | bytes 5341184 | tf_op jit(solution)/shard_map/dot_general | solution.py:44
  152.4 0.0 copy-done.11
  152.4 0.0 copy-start.10
  152.4 2.0 %fusion.32 = f32[4096,128]{1,0:T(8,128)S(1)} fusion(bf16[4096,384]{1,0:T(8,128)(2,1)S(1)} %bitcast.131, bf16[2,9,384,128]{3,2,1,0:T(8,128)(2,1)} %all-gather.2.cloned.1.call-done), kind=kOutput, calls=%fused_computation.54 | convolution fusion | flops 402653184 | bytes 5341184 | tf_op jit(solution)/shard_map/dot_general | solution.py:44
  154.5 2.0 %fusion.33 = f32[4096,128]{1,0:T(8,128)S(1)} fusion(bf16[4096,384]{1,0:T(8,128)(2,1)S(1)} %bitcast.130, bf16[2,9,384,128]{3,2,1,0:T(8,128)(2,1)} %all-gather.2.cloned.1.call-done), kind=kOutput, calls=%fused_computation.56 | convolution fusion | flops 402653184 | bytes 5341184 | tf_op jit(solution)/shard_map/dot_general | solution.py:44
  156.6 2.0 %fusion.34 = f32[4096,128]{1,0:T(8,128)S(1)} fusion(bf16[4096,384]{1,0:T(8,128)(2,1)S(1)} %bitcast.129, bf16[2,9,384,128]{3,2,1,0:T(8,128)(2,1)} %all-gather.2.cloned.1.call-done), kind=kOutput, calls=%fused_computation.58 | convolution fusion | flops 402653184 | bytes 5341184 | tf_op jit(solution)/shard_map/dot_general | solution.py:44
  158.6 2.0 %fusion.35 = f32[4096,128]{1,0:T(8,128)S(1)} fusion(bf16[4096,384]{1,0:T(8,128)(2,1)S(1)} %bitcast.127, bf16[2,9,384,128]{3,2,1,0:T(8,128)(2,1)} %all-gather.2.cloned.1.call-done), kind=kOutput, calls=%fused_computation.60 | convolution fusion | flops 402653184 | bytes 5341184 | tf_op jit(solution)/shard_map/dot_general | solution.py:44
  160.6 2.0 %fusion.36 = f32[4096,128]{1,0:T(8,128)S(1)} fusion(bf16[4096,384]{1,0:T(8,128)(2,1)S(1)} %bitcast.125, bf16[2,9,384,128]{3,2,1,0:T(8,128)(2,1)} %all-gather.2.cloned.1.call-done), kind=kOutput, calls=%fused_computation.62 | convolution fusion | flops 402653184 | bytes 5341184 | tf_op jit(solution)/shard_map/dot_general | solution.py:44
  162.7 0.0 copy-done.4
  162.7 1.9 %fusion.37 = f32[4096,128]{1,0:T(8,128)S(1)} fusion(bf16[4096,384]{1,0:T(8,128)(2,1)S(1)} %bitcast.123, bf16[2,9,384,128]{3,2,1,0:T(8,128)(2,1)} %all-gather.2.cloned.1.call-done), kind=kOutput, calls=%fused_computation.64 | convolution fusion | flops 402653184 | bytes 5341184 | tf_op jit(solution)/shard_map/dot_general | solution.py:44
  164.6 2.0 %fusion.38 = f32[4096,128]{1,0:T(8,128)S(1)} fusion(bf16[4096,384]{1,0:T(8,128)(2,1)S(1)} %bitcast.121, bf16[2,9,384,128]{3,2,1,0:T(8,128)(2,1)} %all-gather.2.cloned.1.call-done), kind=kOutput, calls=%fused_computation.66 | convolution fusion | flops 402653184 | bytes 5341184 | tf_op jit(solution)/shard_map/dot_general | solution.py:44
  166.6 2.5 %fusion.11 = f32[4096,128]{1,0:T(8,128)S(1)} fusion(f32[4096,128]{1,0:T(8,128)S(1)} %fusion.31, f32[4096,128]{1,0:T(8,128)S(1)} %fusion.32, f32[4096,128]{1,0:T(8,128)S(1)} %fusion.33, f32[4096,128]{1,0:T(8,128)S(1)} %fusion.34, f32[4096,128]{1,0:T(8,128)S(1)} %fusion.35, f32[4096,128]{1,0:T(8,128)S(1)} %fusion.36, f32[4096,128]{1,0:T(8,128)S(1)} %fusion.37, ...), kind=kOutput, calls=%fused_computation.17 | convolution fusion | flops 406847488 | bytes 22118400 | tf_op jit(solution)/shard_map/dot_general | solution.py:44
  169.1 1.3 add_convert_fusion
  (12 shorter events, 0.0 us)
Async XLA Ops:
  6.5 66.9 %all-gather.2.cloned.1.call-start = ((), (), s32[]{:S(2)}) async-start(), calls=%async_computation | async-start | bytes 2654208 | tf_op jit(solution)/shard_map/all_gather | solution.py:53
  8.3 25.8 %collective-permute-start = (bf16[2,4,512,128]{3,2,1,0:T(8,128)(2,1)S(1)}, bf16[2,4,512,128]{3,2,1,0:T(8,128)(2,1)S(1)}, u32[]{:S(2)}, u32[]{:S(2)}) collective-permute-start(bf16[2,4,512,128]{3,2,1,0:T(8,128)(2,1)S(1)} %fusion.24), channel_id=1, source_target_pairs={{0,4},{4,8},{8,12},{1,5},{5,9},{9,13},{2,6},{6,10},{10,14},{3,7},{... | collective-permute-start | bytes 3145736 | tf_op jit(solution)/shard_map/ppermute | solution.py:10
  35.2 11.0 %collective-permute-start.1 = (bf16[4,1,512,128]{3,2,1,0:T(8,128)(2,1)}, bf16[4,1,512,128]{3,2,1,0:T(8,128)(2,1)S(1)}, u32[]{:S(2)}, u32[]{:S(2)}) collective-permute-start(bf16[4,1,512,128]{3,2,1,0:T(8,128)(2,1)} %get-tuple-element.29), channel_id=1, source_target_pairs={{0,1},{1,2},{2,3},{4,5},{5,6},{6,7},{8,9},{9,10},{10,11},{12,13},{... | collective-permute-start | bytes 1572872 | tf_op jit(solution)/shard_map/ppermute | solution.py:21
  39.8 10.7 %collective-permute-start.2 = (bf16[4,1,512,128]{3,2,1,0:T(8,128)(2,1)}, bf16[4,1,512,128]{3,2,1,0:T(8,128)(2,1)S(1)}, u32[]{:S(2)}, u32[]{:S(2)}) collective-permute-start(bf16[4,1,512,128]{3,2,1,0:T(8,128)(2,1)} %get-tuple-element.30), channel_id=1, source_target_pairs={{1,0},{2,1},{3,2},{5,4},{6,5},{7,6},{9,8},{10,9},{11,10},{13,12},{... | collective-permute-start | bytes 1572872 | tf_op jit(solution)/shard_map/ppermute | solution.py:23
  73.4 3.0 %copy-start.7 = (bf16[2,4,512,384]{3,2,1,0:T(8,128)(2,1)S(1)}, bf16[2,4,512,384]{3,2,1,0:T(8,128)(2,1)}, u32[]{:S(2)}) copy-start(bf16[2,4,512,384]{3,2,1,0:T(8,128)(2,1)} %get-tuple-element.16) | copy-start | bytes 9437188
  76.5 2.0 %copy-start.5 = (bf16[2,4,512,384]{3,2,1,0:T(8,128)(2,1)S(1)}, bf16[2,4,512,384]{3,2,1,0:T(8,128)(2,1)}, u32[]{:S(2)}) copy-start(bf16[2,4,512,384]{3,2,1,0:T(8,128)(2,1)} %get-tuple-element.17) | copy-start | bytes 9437188
  78.5 2.0 %copy-start.3 = (bf16[2,4,512,384]{3,2,1,0:T(8,128)(2,1)S(1)}, bf16[2,4,512,384]{3,2,1,0:T(8,128)(2,1)}, u32[]{:S(2)}) copy-start(bf16[2,4,512,384]{3,2,1,0:T(8,128)(2,1)} %get-tuple-element.18) | copy-start | bytes 9437188
  80.6 2.0 %copy-start.2 = (bf16[2,4,512,384]{3,2,1,0:T(8,128)(2,1)S(1)}, bf16[2,4,512,384]{3,2,1,0:T(8,128)(2,1)}, u32[]{:S(2)}) copy-start(bf16[2,4,512,384]{3,2,1,0:T(8,128)(2,1)} %get-tuple-element.19) | copy-start | bytes 9437188
  82.6 2.0 %copy-start.1 = (bf16[2,4,512,384]{3,2,1,0:T(8,128)(2,1)S(1)}, bf16[2,4,512,384]{3,2,1,0:T(8,128)(2,1)}, u32[]{:S(2)}) copy-start(bf16[2,4,512,384]{3,2,1,0:T(8,128)(2,1)} %get-tuple-element.20) | copy-start | bytes 9437188
  84.7 2.0 %copy-start = (bf16[2,4,512,384]{3,2,1,0:T(8,128)(2,1)S(1)}, bf16[2,4,512,384]{3,2,1,0:T(8,128)(2,1)}, u32[]{:S(2)}) copy-start(bf16[2,4,512,384]{3,2,1,0:T(8,128)(2,1)} %get-tuple-element.21) | copy-start | bytes 9437188
  88.6 2.0 %copy-start.12 = (bf16[2,4,512,384]{3,2,1,0:T(8,128)(2,1)S(1)}, bf16[2,4,512,384]{3,2,1,0:T(8,128)(2,1)}, u32[]{:S(2)}) copy-start(bf16[2,4,512,384]{3,2,1,0:T(8,128)(2,1)} %get-tuple-element.14) | copy-start | bytes 9437188
  90.6 2.8 %copy-start.14 = (bf16[1,2,4,512,128]{4,3,2,1,0:T(8,128)(2,1)S(1)}, bf16[1,2,4,512,128]{4,3,2,1,0:T(8,128)(2,1)}, u32[]{:S(2)}) copy-start(bf16[1,2,4,512,128]{4,3,2,1,0:T(8,128)(2,1)} %param.2) | copy-start | bytes 3145732
  94.0 25.0 %collective-permute-start.3 = (bf16[2,4,512,128]{3,2,1,0:T(8,128)(2,1)S(1)}, bf16[2,4,512,128]{3,2,1,0:T(8,128)(2,1)S(1)}, u32[]{:S(2)}, u32[]{:S(2)}) collective-permute-start(bf16[2,4,512,128]{3,2,1,0:T(8,128)(2,1)S(1)} %fusion.30), channel_id=1, source_target_pairs={{0,4},{4,8},{8,12},{1,5},{5,9},{9,13},{2,6},{6,10},{10,14},{3,7},{... | collective-permute-start | bytes 3145736 | tf_op jit(solution)/shard_map/ppermute | solution.py:10
  119.1 10.6 %collective-permute-start.4 = (bf16[4,1,512,128]{3,2,1,0:T(8,128)(2,1)S(1)}, bf16[4,1,512,128]{3,2,1,0:T(8,128)(2,1)S(1)}, u32[]{:S(2)}, u32[]{:S(2)}) collective-permute-start(bf16[4,1,512,128]{3,2,1,0:T(8,128)(2,1)S(1)} %get-tuple-element.27), channel_id=1, source_target_pairs={{0,1},{1,2},{2,3},{4,5},{5,6},{6,7},{8,9},{9,10},{10,11},{12,13},{... | collective-permute-start | bytes 1572872 | tf_op jit(solution)/shard_map/ppermute | solution.py:21
  123.6 10.5 %collective-permute-start.5 = (bf16[4,1,512,128]{3,2,1,0:T(8,128)(2,1)S(1)}, bf16[4,1,512,128]{3,2,1,0:T(8,128)(2,1)S(1)}, u32[]{:S(2)}, u32[]{:S(2)}) collective-permute-start(bf16[4,1,512,128]{3,2,1,0:T(8,128)(2,1)S(1)} %get-tuple-element.28), channel_id=1, source_target_pairs={{1,0},{2,1},{3,2},{5,4},{6,5},{7,6},{9,8},{10,9},{11,10},{13,12},{... | collective-permute-start | bytes 1572872 | tf_op jit(solution)/shard_map/ppermute | solution.py:23
  149.4 3.0 %copy-start.11 = (bf16[2,4,512,384]{3,2,1,0:T(8,128)(2,1)S(1)}, bf16[2,4,512,384]{3,2,1,0:T(8,128)(2,1)}, u32[]{:S(2)}) copy-start(bf16[2,4,512,384]{3,2,1,0:T(8,128)(2,1)} %get-tuple-element.7) | copy-start | bytes 9437188
  152.4 2.0 %copy-start.10 = (bf16[2,4,512,384]{3,2,1,0:T(8,128)(2,1)S(1)}, bf16[2,4,512,384]{3,2,1,0:T(8,128)(2,1)}, u32[]{:S(2)}) copy-start(bf16[2,4,512,384]{3,2,1,0:T(8,128)(2,1)} %get-tuple-element.8) | copy-start | bytes 9437188
  154.5 2.0 %copy-start.9 = (bf16[2,4,512,384]{3,2,1,0:T(8,128)(2,1)S(1)}, bf16[2,4,512,384]{3,2,1,0:T(8,128)(2,1)}, u32[]{:S(2)}) copy-start(bf16[2,4,512,384]{3,2,1,0:T(8,128)(2,1)} %get-tuple-element.9) | copy-start | bytes 9437188
  156.5 2.0 %copy-start.8 = (bf16[2,4,512,384]{3,2,1,0:T(8,128)(2,1)S(1)}, bf16[2,4,512,384]{3,2,1,0:T(8,128)(2,1)}, u32[]{:S(2)}) copy-start(bf16[2,4,512,384]{3,2,1,0:T(8,128)(2,1)} %get-tuple-element.10) | copy-start | bytes 9437188
  158.6 2.0 %copy-start.6 = (bf16[2,4,512,384]{3,2,1,0:T(8,128)(2,1)S(1)}, bf16[2,4,512,384]{3,2,1,0:T(8,128)(2,1)}, u32[]{:S(2)}) copy-start(bf16[2,4,512,384]{3,2,1,0:T(8,128)(2,1)} %get-tuple-element.11) | copy-start | bytes 9437188
  160.6 2.0 %copy-start.4 = (bf16[2,4,512,384]{3,2,1,0:T(8,128)(2,1)S(1)}, bf16[2,4,512,384]{3,2,1,0:T(8,128)(2,1)}, u32[]{:S(2)}) copy-start(bf16[2,4,512,384]{3,2,1,0:T(8,128)(2,1)} %get-tuple-element.12) | copy-start | bytes 9437188
  164.6 2.0 %copy-start.13 = (bf16[2,4,512,384]{3,2,1,0:T(8,128)(2,1)S(1)}, bf16[2,4,512,384]{3,2,1,0:T(8,128)(2,1)}, u32[]{:S(2)}) copy-start(bf16[2,4,512,384]{3,2,1,0:T(8,128)(2,1)} %get-tuple-element.5) | copy-start | bytes 9437188
Sparse Core Ops, SparseCore 0:
  41.9 31.4 all-gather.1
where the time goes:
time: 178 us; the launch traced here: 177 us
  waiting for transfers between devices  68.5 us (38%)
  matrix products  39.3 us (22%)
  local copies, waits for them, and re-layouts  23.3 us (13%)
  starting transfers between devices  20.2 us (11%)
  between operations  13.9 us (8%)
  other arithmetic  12 us (7%)
    ppermute x2, waiting for transfers between devices, from_behind(): return lax.ppermute(block, axis, route)  43.5 us
    dot_general x18, matrix products, conv_block(): jnp.dot(slab.reshape(-1, 3 * chans), taps[time_tap * 3 + row_tap], prefer...  39.3 us
    slice x2, local copies, waits for them, and re-layouts, conv_block(): slab = joined[time_tap:time_tap + frames, row_tap:row_tap + rows]  18.6 us
    ppermute x2, starting transfers between devices, padded_2(): lax.ppermute(tail, axis, [(i, (i + 1) % count) for i in range(ends)])  9.08 us
    ppermute x2, waiting for transfers between devices, padded_2(): lax.ppermute(head, axis, [((i + 1) % count, i) for i in range(ends)])  8.69 us
    ppermute x2, waiting for transfers between devices, padded_2(): lax.ppermute(tail, axis, [(i, (i + 1) % count) for i in range(ends)])  8.64 us
    all_gather x1, waiting for transfers between devices, body(): all_taps = lax.all_gather(weights, 'section', axis=0, tiled=True)  7.69 us
    ppermute x2, starting transfers between devices, from_behind(): return lax.ppermute(block, axis, route)  7.29 us
  transfers between devices with their start and end apart: 7, of which 7 were waited for; matrix products, arithmetic and copies ran while one was open for 9% of the time, Pallas kernels for 0%

commit v1 on v0

--- a/solution.py
+++ b/solution.py
@@ -33,31 +33,23 @@
     carried = from_behind(act, "tm", 1)
     extended = jnp.concatenate([carried, act], axis=0)
     padded = padded_2(extended, (("space", 1),), 1)
-    padded = jnp.pad(padded, ((0, 0), (0, 0), (1, 1), (0, 0)))
-    joined = jnp.concatenate(
-        [padded[:, :, 0:width], padded[:, :, 1 : width + 1], padded[:, :, 2 : width + 2]], axis=-1
-    )
-    total = jnp.zeros((frames * rows * width, chans), jnp.float32)
-    for time_tap in range(3):
-        for row_tap in range(3):
-            slab = joined[time_tap : time_tap + frames, row_tap : row_tap + rows]
-            total = total + jnp.dot(
-                slab.reshape(-1, 3 * chans),
-                taps[time_tap * 3 + row_tap],
-                preferred_element_type=jnp.float32,
-            )
-    return (clip.astype(jnp.float32) + total.reshape(clip.shape)).astype(jnp.bfloat16)
+    kernel = taps.reshape(3, 3, 3, chans, chans)
+    total = lax.conv_general_dilated(
+        padded[None],
+        kernel,
+        window_strides=(1, 1, 1),
+        padding=((0, 0), (0, 0), (1, 1)),
+        dimension_numbers=("NDHWC", "DHWIO", "NDHWC"),
+        preferred_element_type=jnp.float32,
+    )[0]
+    return (clip.astype(jnp.float32) + total).astype(jnp.bfloat16)
 
 
 def body(video, weights):
     all_taps = lax.all_gather(weights, "section", axis=0, tiled=True)
-    first_taps = all_taps[0]
-    second_taps = all_taps[1]
-    index = 0
-    hiddens = [conv_block(video[index], first_taps)]
-    index = 0
-    finished = [conv_block(hiddens[index], second_taps)]
-    return jnp.stack(finished, axis=0)
+    hidden = conv_block(video[0], all_taps[0])
+    finished = conv_block(hidden, all_taps[1])
+    return finished[None]
 
 
 def solution(mesh):

time: 178 us -> 128 us (0.72)
  matrix products: 39.3 us -> 16.4 us
  waiting for transfers between devices: 68.5 us -> 50.5 us
  local copies, waits for them, and re-layouts: 23.3 us -> 10.5 us
  other arithmetic: 12 us -> 16.2 us
    dot_general x18 -> x0, matrix products: 39.3 us -> none  [conv_block(): jnp.dot(slab.reshape(-1, 3 * chans), taps[time_tap * 3 + row_tap], prefer...]
    slice x4 -> x5, local copies, waits for them, and re-layouts: 23.2 us -> 1.86 us  [the longest x1 1.58 us: body(): hidden = conv_block(video[0], all_taps[0])]
    conv_general_dilated x0 -> x2, matrix products: none -> 16.4 us  [conv_block(): lax.conv_general_dilated(padded[None], kernel, window_strides=(1, 1, 1),...]
    ppermute x2, waiting for transfers between devices: 8.64 us -> 0.89 us  [padded_2(): lax.ppermute(tail, axis, [(i, (i + 1) % count) for i in range(ends)])]
    all_gather x1, waiting for transfers between devices: 7.69 us -> 0.02 us  [body(): all_taps = lax.all_gather(weights, 'section', axis=0, tiled=True)]
    broadcast_in_dim x0 -> x2, other arithmetic: none -> 7.59 us  [conv_block(): padded[None]]
    ppermute x2, waiting for transfers between devices: 43.5 us -> 39.9 us  [from_behind(): return lax.ppermute(block, axis, route)]
    concatenate x4 -> x2, other arithmetic: 7.21 us -> 3.63 us  [conv_block(): extended = jnp.concatenate([carried, act], axis=0)]
  transfers between devices with their start and end apart: 7 -> 7, of which waited for: 7 -> 6; matrix products, arithmetic and copies ran while one was open for 9% -> 8% of each run, Pallas kernels for 0% -> 0%
where the time goes in v1:
time: 128 us; the launch traced here: 127 us
  waiting for transfers between devices  50.5 us (39%)
  starting transfers between devices  20.3 us (16%)
  matrix products  16.4 us (13%)
  other arithmetic  16.2 us (13%)
  between operations  13.6 us (11%)
  local copies, waits for them, and re-layouts  10.5 us (8%)
    ppermute x2, waiting for transfers between devices, from_behind(): return lax.ppermute(block, axis, route)  39.9 us
    conv_general_dilated x2, matrix products, conv_block(): lax.conv_general_dilated(padded[None], kernel, window_strides=(1, 1, 1),...  16.4 us
    ppermute x2, waiting for transfers between devices, padded_2(): lax.ppermute(head, axis, [((i + 1) % count, i) for i in range(ends)])  9.69 us
    ppermute x2, starting transfers between devices, from_behind(): return lax.ppermute(block, axis, route)  8.26 us
    broadcast_in_dim x2, other arithmetic, conv_block(): padded[None]  7.59 us
    ppermute x2, starting transfers between devices, padded_2(): lax.ppermute(tail, axis, [(i, (i + 1) % count) for i in range(ends)])  6.69 us
    ppermute x2, starting transfers between devices, padded_2(): lax.ppermute(head, axis, [((i + 1) % count, i) for i in range(ends)])  5.37 us
    convert_element_type x2, other arithmetic, conv_block(): act = jax.nn.silu(clip.astype(jnp.float32)).astype(jnp.bfloat16)  3.65 us
  transfers between devices with their start and end apart: 7, of which 6 were waited for; matrix products, arithmetic and copies ran while one was open for 8% of the time, Pallas kernels for 0%

profile of v1, /device:TPU:1, one launch (start us, length us, event | category | flops | bytes accessed | tf_op | source)
XLA Modules:
  0.0 127.5 jit_solution(328507993011063070)
XLA Ops:
  6.5 0.0 all-gather.2.cloned.1.call-start
  6.5 2.4 %fusion.21 = bf16[2,4,512,128]{3,1,2,0:T(4,128)(2,1)S(1)} fusion(bf16[1,2,4,512,128]{4,3,2,1,0:T(8,128)(2,1)} %param.2), kind=kLoop, calls=%fused_computation.26 | loop fusion | flops 3145728 | bytes 2097152 | tf_op jit(solution)/shard_map/convert_element_type | solution.py:32
  8.9 4.1 %collective-permute-start = (bf16[2,4,512,128]{3,1,2,0:T(4,128)(2,1)S(1)}, bf16[2,4,512,128]{3,1,2,0:T(4,128)(2,1)S(1)}, u32[]{:S(2)}, u32[]{:S(2)}) collective-permute-start(bf16[2,4,512,128]{3,1,2,0:T(4,128)(2,1)S(1)} %fusion.21), channel_id=1, source_target_pairs={{0,4},{4,8},{8,12},{1,5},{5,9},{9,13},{2,6},{6,10},{10,14},{3,7},{... | collective-permute-start | bytes 3145736 | tf_op jit(solution)/shard_map/ppermute | solution.py:10
  13.0 0.0 all-gather.2.cloned.1.call-update
  13.1 21.7 %collective-permute-done = bf16[2,4,512,128]{3,1,2,0:T(4,128)(2,1)S(1)} collective-permute-done((bf16[2,4,512,128]{3,1,2,0:T(4,128)(2,1)S(1)}, bf16[2,4,512,128]{3,1,2,0:T(4,128)(2,1)S(1)}, u32[]{:S(2)}, u32[]{:S(2)}) %collective-permute-start) | collective-permute-done | bytes 1048608 | tf_op jit(solution)/shard_map/ppermute | solution.py:10
  34.8 1.8 %fusion.38 = (bf16[4,1,512,128]{3,1,2,0:T(2,128)(2,1)S(1)}, bf16[4,1,512,128]{3,1,2,0:T(2,128)(2,1)S(1)}) fusion(bf16[2,4,512,128]{3,1,2,0:T(4,128)(2,1)S(1)} %collective-permute-done, bf16[2,4,512,128]{3,1,2,0:T(4,128)(2,1)S(1)} %fusion.21), kind=kLoop, calls=%fused_computation.44 | loop fusion | flops 2097152 | bytes 3145728 | tf_op jit(solution)/shard_map/concatenate | solution.py:34
  36.6 0.1 copy.15
  36.7 3.5 %collective-permute-start.2 = (bf16[4,1,512,128]{3,2,1,0:T(8,128)(2,1)S(1)}, bf16[4,1,512,128]{3,2,1,0:T(8,128)(2,1)S(1)}, u32[]{:S(2)}, u32[]{:S(2)}) collective-permute-start(bf16[4,1,512,128]{3,2,1,0:T(8,128)(2,1)S(1)} %copy.15), channel_id=1, source_target_pairs={{1,0},{2,1},{3,2},{5,4},{6,5},{7,6},{9,8},{10,9},{11,10},{13,12},{... | collective-permute-start | bytes 1572872 | tf_op jit(solution)/shard_map/ppermute | solution.py:23
  40.2 0.1 copy.14
  40.2 3.0 %collective-permute-start.1 = (bf16[4,1,512,128]{3,2,1,0:T(8,128)(2,1)S(1)}, bf16[4,1,512,128]{3,2,1,0:T(8,128)(2,1)S(1)}, u32[]{:S(2)}, u32[]{:S(2)}) collective-permute-start(bf16[4,1,512,128]{3,2,1,0:T(8,128)(2,1)S(1)} %copy.14), channel_id=1, source_target_pairs={{0,1},{1,2},{2,3},{4,5},{5,6},{6,7},{8,9},{9,10},{10,11},{12,13},{... | collective-permute-start | bytes 1572872 | tf_op jit(solution)/shard_map/ppermute | solution.py:21
  43.3 4.8 %collective-permute-done.2 = bf16[4,1,512,128]{3,2,1,0:T(8,128)(2,1)S(1)} collective-permute-done((bf16[4,1,512,128]{3,2,1,0:T(8,128)(2,1)S(1)}, bf16[4,1,512,128]{3,2,1,0:T(8,128)(2,1)S(1)}, u32[]{:S(2)}, u32[]{:S(2)}) %collective-permute-start.2) | collective-permute-done | bytes 524320 | tf_op jit(solution)/shard_map/ppermute | solution.py:23
  48.1 0.8 copy.17
  48.9 0.4 collective-permute-done.1
  49.4 0.8 copy.16
  50.2 3.9 %maximum_bitcast_fusion = bf16[4,6,1,512,128]{4,1,3,0,2:T(8,128)(2,1)S(1)} fusion(bf16[4,1,512,128]{3,1,2,0:T(2,128)(2,1)S(1)} %copy.17, bf16[2,4,512,128]{3,1,2,0:T(4,128)(2,1)S(1)} %fusion.21, bf16[2,4,512,128]{3,1,2,0:T(4,128)(2,1)S(1)} %collective-permute-done, bf16[4,1,512,128]{3,1,2,0:T(2,128)(2,1)S(1)} %copy.16), kind=kLoop, calls=%fused_computation.3 | loop fusion | flops 12582912 | bytes 6291456 | tf_op jit(solution)/shard_map/broadcast_in_dim | solution.py:38
  54.1 0.8 pad
  54.9 0.4 copy.20
  55.3 0.0 copy-start.1
  55.4 0.0 all-gather.2.cloned.1.call-done
  55.4 1.6 %fusion.45 = (bf16[1,9,384,128]{3,2,1,0:T(8,128)(2,1)S(1)}, bf16[1,9,384,128]{3,2,1,0:T(8,128)(2,1)S(1)}) fusion(bf16[2,9,384,128]{3,2,1,0:T(8,128)(2,1)} %all-gather.2.cloned.1.call-done), kind=kLoop, calls=%fused_computation.53 | loop fusion | bytes 3538944 | tf_op jit(solution)/shard_map/slice | solution.py:50
  57.0 0.0 copy-done.1
  57.0 8.3 %fusion.34 = f32[2,4,8,65,128]{4,2,3,1,0:T(8,128)S(1)} fusion(bf16[3,3,3,128,128]{4,3,2,1,0:T(8,128)(2,1)S(1)} %bitcast.62, bf16[4,6,1,7,2,128]{5,3,4,1,0,2:T(8,128)(2,1)S(1)} %slice.30, bf16[4,6,1,8,65,128]{5,3,4,1,0,2:T(8,128)(2,1)S(1)} %copy.20, pred[8,65]{0,1:T(8,128)(4,1)S(1)} %copy-done.1), kind=kOutput, calls=%fused_computation.42 | convolution fusion | flops 3690913792 | bytes 6296072 | tf_op jit(solution)/shard_map/conv_general_dilated | solution.py:37
  65.3 0.0 copy-start
  65.3 0.5 copy.21
  65.9 0.7 copy-done
  66.5 1.3 fusion.26
  67.8 4.2 %collective-permute-start.3 = (bf16[2,4,512,128]{3,1,2,0:T(4,128)(2,1)S(1)}, bf16[2,4,512,128]{3,1,2,0:T(4,128)(2,1)S(1)}, u32[]{:S(2)}, u32[]{:S(2)}) collective-permute-start(bf16[2,4,512,128]{3,1,2,0:T(4,128)(2,1)S(1)} %fusion.26), channel_id=1, source_target_pairs={{0,4},{4,8},{8,12},{1,5},{5,9},{9,13},{2,6},{6,10},{10,14},{3,7},{... | collective-permute-start | bytes 3145736 | tf_op jit(solution)/shard_map/ppermute | solution.py:10
  72.0 18.1 %collective-permute-done.3 = bf16[2,4,512,128]{3,1,2,0:T(4,128)(2,1)S(1)} collective-permute-done((bf16[2,4,512,128]{3,1,2,0:T(4,128)(2,1)S(1)}, bf16[2,4,512,128]{3,1,2,0:T(4,128)(2,1)S(1)}, u32[]{:S(2)}, u32[]{:S(2)}) %collective-permute-start.3) | collective-permute-done | bytes 1048608 | tf_op jit(solution)/shard_map/ppermute | solution.py:10
  90.1 1.8 %fusion.37 = (bf16[4,1,512,128]{3,1,2,0:T(2,128)(2,1)S(1)}, bf16[4,1,512,128]{3,1,2,0:T(2,128)(2,1)S(1)}) fusion(bf16[2,4,512,128]{3,1,2,0:T(4,128)(2,1)S(1)} %collective-permute-done.3, bf16[2,4,512,128]{3,1,2,0:T(4,128)(2,1)S(1)} %fusion.26), kind=kLoop, calls=%fused_computation.43 | loop fusion | flops 2097152 | bytes 3145728 | tf_op jit(solution)/shard_map/concatenate | solution.py:34
  91.9 0.1 copy.23
  92.0 1.9 %collective-permute-start.5 = (bf16[4,1,512,128]{3,2,1,0:T(8,128)(2,1)S(1)}, bf16[4,1,512,128]{3,2,1,0:T(8,128)(2,1)S(1)}, u32[]{:S(2)}, u32[]{:S(2)}) collective-permute-start(bf16[4,1,512,128]{3,2,1,0:T(8,128)(2,1)S(1)} %copy.23), channel_id=1, source_target_pairs={{1,0},{2,1},{3,2},{5,4},{6,5},{7,6},{9,8},{10,9},{11,10},{13,12},{... | collective-permute-start | bytes 1572872 | tf_op jit(solution)/shard_map/ppermute | solution.py:23
  93.9 0.1 copy.22
  94.0 3.6 %collective-permute-start.4 = (bf16[4,1,512,128]{3,2,1,0:T(8,128)(2,1)S(1)}, bf16[4,1,512,128]{3,2,1,0:T(8,128)(2,1)S(1)}, u32[]{:S(2)}, u32[]{:S(2)}) collective-permute-start(bf16[4,1,512,128]{3,2,1,0:T(8,128)(2,1)S(1)} %copy.22), channel_id=1, source_target_pairs={{0,1},{1,2},{2,3},{4,5},{5,6},{6,7},{8,9},{9,10},{10,11},{12,13},{... | collective-permute-start | bytes 1572872 | tf_op jit(solution)/shard_map/ppermute | solution.py:21
  97.7 4.8 %collective-permute-done.5 = bf16[4,1,512,128]{3,2,1,0:T(8,128)(2,1)S(1)} collective-permute-done((bf16[4,1,512,128]{3,2,1,0:T(8,128)(2,1)S(1)}, bf16[4,1,512,128]{3,2,1,0:T(8,128)(2,1)S(1)}, u32[]{:S(2)}, u32[]{:S(2)}) %collective-permute-start.5) | collective-permute-done | bytes 524320 | tf_op jit(solution)/shard_map/ppermute | solution.py:23
  102.5 0.8 copy.25
  103.3 0.4 collective-permute-done.4
  103.8 0.8 copy.24
  104.6 3.7 %maximum_bitcast_fusion.1 = bf16[4,6,1,512,128]{4,1,3,0,2:T(8,128)(2,1)S(1)} fusion(bf16[4,1,512,128]{3,1,2,0:T(2,128)(2,1)S(1)} %copy.25, bf16[2,4,512,128]{3,1,2,0:T(4,128)(2,1)S(1)} %fusion.26, bf16[2,4,512,128]{3,1,2,0:T(4,128)(2,1)S(1)} %collective-permute-done.3, bf16[4,1,512,128]{3,1,2,0:T(2,128)(2,1)S(1)} %copy.24), kind=kLoop, calls=%fused_computation.4 | loop fusion | flops 12582912 | bytes 6291456 | tf_op jit(solution)/shard_map/broadcast_in_dim | solution.py:38
  108.3 0.8 pad.2
  109.1 0.4 copy.28
  109.6 8.1 %fusion.31 = f32[2,4,8,65,128]{4,2,3,1,0:T(8,128)S(1)} fusion(bf16[3,3,3,128,128]{4,3,2,1,0:T(8,128)(2,1)S(1)} %bitcast.61, bf16[4,6,1,7,2,128]{5,3,4,1,0,2:T(8,128)(2,1)S(1)} %slice.35, bf16[4,6,1,8,65,128]{5,3,4,1,0,2:T(8,128)(2,1)S(1)} %copy.28, pred[8,65]{0,1:T(8,128)(4,1)S(1)} %copy-done.1), kind=kOutput, calls=%fused_computation.41 | convolution fusion | flops 3690913792 | bytes 6296072 | tf_op jit(solution)/shard_map/conv_general_dilated | solution.py:37
  117.7 0.5 copy.29
  118.2 1.3 %fusion.28 = bf16[1,2,4,512,128]{4,2,3,1,0:T(4,128)(2,1)S(1)} fusion(f32[2,4,1,520,128]{4,1,3,0,2:T(4,128)S(1)} %bitcast.60, f32[2,4,1,520,128]{4,1,3,0,2:T(4,128)S(1)} %bitcast.57, bf16[1,2,4,512,128]{4,3,2,1,0:T(8,128)(2,1)S(1)} %copy-done), kind=kLoop, calls=%fused_computation.34 | loop fusion | flops 3145728 | bytes 6291456 | tf_op jit(solution)/shard_map/convert_element_type | solution.py:45
  119.5 1.1 copy.30
  (2 shorter events, 0.1 us)
Async XLA Ops:
  6.5 48.9 %all-gather.2.cloned.1.call-start = ((), (), s32[]{:S(2)}) async-start(), calls=%async_computation | async-start | bytes 2654208 | tf_op jit(solution)/shard_map/all_gather | solution.py:49
  8.9 25.8 %collective-permute-start = (bf16[2,4,512,128]{3,1,2,0:T(4,128)(2,1)S(1)}, bf16[2,4,512,128]{3,1,2,0:T(4,128)(2,1)S(1)}, u32[]{:S(2)}, u32[]{:S(2)}) collective-permute-start(bf16[2,4,512,128]{3,1,2,0:T(4,128)(2,1)S(1)} %fusion.21), channel_id=1, source_target_pairs={{0,4},{4,8},{8,12},{1,5},{5,9},{9,13},{2,6},{6,10},{10,14},{3,7},{... | collective-permute-start | bytes 3145736 | tf_op jit(solution)/shard_map/ppermute | solution.py:10
  36.7 11.4 %collective-permute-start.2 = (bf16[4,1,512,128]{3,2,1,0:T(8,128)(2,1)S(1)}, bf16[4,1,512,128]{3,2,1,0:T(8,128)(2,1)S(1)}, u32[]{:S(2)}, u32[]{:S(2)}) collective-permute-start(bf16[4,1,512,128]{3,2,1,0:T(8,128)(2,1)S(1)} %copy.15), channel_id=1, source_target_pairs={{1,0},{2,1},{3,2},{5,4},{6,5},{7,6},{9,8},{10,9},{11,10},{13,12},{... | collective-permute-start | bytes 1572872 | tf_op jit(solution)/shard_map/ppermute | solution.py:23
  40.2 9.2 %collective-permute-start.1 = (bf16[4,1,512,128]{3,2,1,0:T(8,128)(2,1)S(1)}, bf16[4,1,512,128]{3,2,1,0:T(8,128)(2,1)S(1)}, u32[]{:S(2)}, u32[]{:S(2)}) collective-permute-start(bf16[4,1,512,128]{3,2,1,0:T(8,128)(2,1)S(1)} %copy.14), channel_id=1, source_target_pairs={{0,1},{1,2},{2,3},{4,5},{5,6},{6,7},{8,9},{9,10},{10,11},{12,13},{... | collective-permute-start | bytes 1572872 | tf_op jit(solution)/shard_map/ppermute | solution.py:21
  55.3 1.7 %copy-start.1 = (pred[8,65]{0,1:T(8,128)(4,1)S(1)}, pred[8,65]{0,1:T(8,128)(4,1)}, u32[]{:S(2)}) copy-start(pred[8,65]{0,1:T(8,128)(4,1)} %constant.14) | copy-start | bytes 1564
  65.3 1.2 copy-start
  67.8 22.3 %collective-permute-start.3 = (bf16[2,4,512,128]{3,1,2,0:T(4,128)(2,1)S(1)}, bf16[2,4,512,128]{3,1,2,0:T(4,128)(2,1)S(1)}, u32[]{:S(2)}, u32[]{:S(2)}) collective-permute-start(bf16[2,4,512,128]{3,1,2,0:T(4,128)(2,1)S(1)} %fusion.26), channel_id=1, source_target_pairs={{0,4},{4,8},{8,12},{1,5},{5,9},{9,13},{2,6},{6,10},{10,14},{3,7},{... | collective-permute-start | bytes 3145736 | tf_op jit(solution)/shard_map/ppermute | solution.py:10
  92.0 10.5 %collective-permute-start.5 = (bf16[4,1,512,128]{3,2,1,0:T(8,128)(2,1)S(1)}, bf16[4,1,512,128]{3,2,1,0:T(8,128)(2,1)S(1)}, u32[]{:S(2)}, u32[]{:S(2)}) collective-permute-start(bf16[4,1,512,128]{3,2,1,0:T(8,128)(2,1)S(1)} %copy.23), channel_id=1, source_target_pairs={{1,0},{2,1},{3,2},{5,4},{6,5},{7,6},{9,8},{10,9},{11,10},{13,12},{... | collective-permute-start | bytes 1572872 | tf_op jit(solution)/shard_map/ppermute | solution.py:23
  94.0 9.8 %collective-permute-start.4 = (bf16[4,1,512,128]{3,2,1,0:T(8,128)(2,1)S(1)}, bf16[4,1,512,128]{3,2,1,0:T(8,128)(2,1)S(1)}, u32[]{:S(2)}, u32[]{:S(2)}) collective-permute-start(bf16[4,1,512,128]{3,2,1,0:T(8,128)(2,1)S(1)} %copy.22), channel_id=1, source_target_pairs={{0,1},{1,2},{2,3},{4,5},{5,6},{6,7},{8,9},{9,10},{10,11},{12,13},{... | collective-permute-start | bytes 1572872 | tf_op jit(solution)/shard_map/ppermute | solution.py:21
Sparse Core Ops, SparseCore 0:
  13.2 29.8 all-gather.1
